TPU v7x, 512 devices: a whole 4x8x8 slice. The times are simulated.
512 devices in a mesh: dp: 32 (over y, x), section: 4 (over z_hi), space: 4 (over z_lo, core).
Axes of the slice: x: 4, y: 8, z: 8 (z_hi: 4, z_lo: 2; z = z_hi * 2 + z_lo), core: 2. Of those that a mesh axis runs over, the one named last changes fastest.
Arguments:
- images: bfloat16 [64, 4, 64, 256], P('dp', 'space'), may hold values from -6 to 6
- steps: int32 [64], P('dp'), may hold values from 0 to 999
- out_grad: bfloat16 [64, 4, 64, 256], P('dp', 'space'), may hold values from -0.125 to 0.125
- conv_weight: bfloat16 [4, 3, 3, 256, 256], P('section'), may hold values from -0.125 to 0.125
- gn_gain: float32 [4, 256], P('section'), may hold values from 0.5 to 2
- emb_weight: bfloat16 [4, 256, 512], P('section'), may hold values from -0.375 to 0.375
Outputs:
- grad_conv: float32 [4, 3, 3, 256, 256], P('section')
- grad_gain: float32 [4, 256], P('section')
- grad_emb: float32 [4, 256, 512], P('section')
All inputs are finite; a program needn't handle non-finite values.
Results may differ from a plain program's by a relative error of at most 0.0064.
Values may be sent and summed in bfloat16 or wider, within the bound.
No kernel may reach another device: no remote copies, remote signals or barrier semaphores. Data moves between devices by JAX's collectives and lax.ppermute only.
A program may use at most 64 MiB of HBM per device.

v0:
```python
import math
import jax
import jax.numpy as jnp
from jax import lax
from jax.sharding import Mesh, PartitionSpec as P

G = 32
FREQ = 256
MICRO = 2
EPS = 1e-05


def from_behind(value, axis, steps):
    count = lax.axis_size(axis)
    initial, last = (max(0, -steps), min(count, count - steps))
    return lax.ppermute(value, axis, [(source, source + steps) for source in range(initial, last)])


def extended(shard, sides, width):
    for axis, dim in sides:
        size, length = (lax.axis_size(axis), shard.shape[dim])
        up = [(i, (i + 1) % size) for i in range(size - 1)]
        down = [(j, i) for i, j in up]
        last = lax.slice_in_dim(shard, length - width, length, axis=dim)
        initial = lax.slice_in_dim(shard, 0, width, axis=dim)
        before = lax.ppermute(last, axis, up)
        after = lax.ppermute(initial, axis, down)
        shard = jnp.concatenate([before, shard, after], axis=dim)
    return shard


def sinusoid(timesteps, feature_n):
    half_n = feature_n // 2
    freqs = jnp.exp(-math.log(10000.0) * jnp.arange(half_n, dtype=jnp.float32) / half_n)
    angles = timesteps.astype(jnp.float32)[:, None] * freqs[None, :]
    return jnp.concatenate([jnp.cos(angles), jnp.sin(angles)], axis=1)


def group_sums(tensor, groups):
    batch_n, height_n, width_n, channels = tensor.shape
    split = tensor.reshape(batch_n, height_n, width_n, groups, channels // groups)
    return (jnp.sum(split, axis=(1, 2, 4)), jnp.sum(split * split, axis=(1, 2, 4)))


def spread(values, channels):
    return jnp.repeat(values, channels // values.shape[1], axis=1)[:, None, None, :]


def normalize(tensor, first_sum, square_sum, gains, scales, shifts, cell_count):
    channels = tensor.shape[3]
    average = first_sum / cell_count
    inverse = lax.rsqrt(square_sum / cell_count - average * average + EPS)
    normed = (tensor - spread(average, channels)) * spread(inverse, channels) * gains
    return normed * (1.0 + scales[:, None, None, :]) + shifts[:, None, None, :]


def patches(padded, height_n, width_n):
    return jnp.concatenate(
        [
            padded[:, vertical : vertical + height_n, lateral : lateral + width_n, :]
            for vertical in range(3)
            for lateral in range(3)
        ],
        axis=3,
    )


def convolve(padded, matrix):
    batch_n, height_p, width_p, channels = padded.shape
    flat = patches(padded, height_p - 2, width_p - 2).reshape(-1, 9 * channels)
    return jnp.dot(flat, matrix, preferred_element_type=jnp.float32).reshape(
        batch_n, height_p - 2, width_p - 2, matrix.shape[1]
    )


def flip_weight(weight):
    channels = weight.shape[2]
    return jnp.transpose(weight[::-1, ::-1], (0, 1, 3, 2)).reshape(9 * channels, channels)


def silu_slope(pre_act):
    sigmoid_v = jax.nn.sigmoid(pre_act)
    return sigmoid_v * (1.0 + pre_act * (1.0 - sigmoid_v))


def pad_columns(tensor):
    return jnp.pad(tensor, ((0, 0), (0, 0), (1, 1), (0, 0)))


def pick(stacked, index):
    return lax.dynamic_index_in_dim(stacked, index, 0, keepdims=False)


def norm_backward(tensor, first_sum, square_sum, gains, scales, shifts, cell_count, d_pre):

    def mapping(tensor_v, first_v, square_v, gains_v, scales_v, shifts_v):
        return normalize(tensor_v, first_v, square_v, gains_v, scales_v, shifts_v, cell_count)

    _, pull_back = jax.vjp(mapping, tensor, first_sum, square_sum, gains, scales, shifts)
    return pull_back(d_pre)


def pad_both(tensor):
    return jnp.pad(tensor, ((0, 0), (1, 1), (1, 1), (0, 0)))


def block_forward(inputs, flat_weight, gains, scales, shifts, cell_count):
    tensor = inputs.astype(jnp.float32)
    first_sum, square_sum = group_sums(tensor, G)
    pre_act = normalize(tensor, first_sum, square_sum, gains, scales, shifts, cell_count)
    activation = jax.nn.silu(pre_act).astype(jnp.bfloat16)
    padded = pad_both(activation)
    output = (tensor + convolve(padded, flat_weight)).astype(jnp.bfloat16)
    return (output, (first_sum, square_sum, padded))


def block_backward(upstream, inputs, saved, flipped, gains, scales, shifts, cell_count):
    first_sum, square_sum, _ = saved
    channels = inputs.shape[3]
    tensor = inputs.astype(jnp.float32)
    pre_act = normalize(tensor, first_sum, square_sum, gains, scales, shifts, cell_count)
    d_act = convolve(pad_both(upstream), flipped)
    d_pre = d_act * silu_slope(pre_act)
    d_tensor, d_first, d_square, d_gains, d_scales, d_shifts = norm_backward(
        tensor, first_sum, square_sum, gains, scales, shifts, cell_count, d_pre
    )
    d_tensor = d_tensor + spread(d_first, channels) + 2.0 * tensor * spread(d_square, channels)
    d_input = (upstream.astype(jnp.float32) + d_tensor).astype(jnp.bfloat16)
    return (d_input, (d_gains, d_scales, d_shifts))


def keep(flag, new, old):
    return jax.tree.map(lambda a, b: jnp.where(flag, a, b), new, old)


def per_device(images, steps, out_grad, conv_weight, gn_gain, emb_weight):
    section_count = lax.axis_size("section")
    section_no = lax.axis_index("section")
    images = lax.all_gather(images, "space", axis=1, tiled=True)
    out_grad = lax.all_gather(out_grad, "space", axis=1, tiled=True)
    row_count = images.shape[1]
    col_count = images.shape[2]
    channels = images.shape[3]
    cell_count = row_count * col_count * (channels // G)
    weight = conv_weight[0]
    flat_weight = weight.reshape(9 * channels, channels)
    flipped = flip_weight(weight)
    gains = gn_gain[0]
    features = sinusoid(steps, FREQ)
    embedded = jnp.dot(features, emb_weight[0].astype(jnp.float32), precision=lax.Precision.HIGHEST)
    scales = embedded[:, :channels]
    shifts = embedded[:, channels:]
    last = section_count - 1
    carried = images
    kept = None
    for moment in range(section_count):
        inputs = images
        if moment > 0:
            inputs = lax.ppermute(carried, "section", [(moment - 1, moment)])
        if moment == last:
            inputs = (inputs.astype(jnp.float32) + skip.astype(jnp.float32)).astype(jnp.bfloat16)
        output, saved = block_forward(inputs, flat_weight, gains, scales, shifts, cell_count)
        if moment == 0:
            skip = lax.ppermute(output, "section", [(0, last)])
        state = (inputs, saved)
        kept = state if kept is None else keep(section_no == moment, state, kept)
        carried = output
    kept_in, kept_saved = kept
    carried = out_grad
    kept = None
    for moment in range(section_count):
        active = last - moment
        upstream = out_grad
        if moment > 0:
            upstream = lax.ppermute(carried, "section", [(active + 1, active)])
        if active == 0:
            upstream = (upstream.astype(jnp.float32) + skip_grad.astype(jnp.float32)).astype(
                jnp.bfloat16
            )
        d_input, pieces = block_backward(
            upstream, kept_in, kept_saved, flipped, gains, scales, shifts, cell_count
        )
        if moment == 0:
            skip_grad = lax.ppermute(d_input, "section", [(last, 0)])
        state = (upstream, pieces)
        kept = state if kept is None else keep(section_no == active, state, kept)
        carried = d_input
    kept_up, (d_gains, d_scales, d_shifts) = kept
    space_count = lax.axis_size("space")
    space_no = lax.axis_index("space")
    patch_rows = 9 * channels // space_count
    flat_patch = patches(kept_saved[2], row_count, col_count).reshape(-1, 9 * channels)
    own_patch = lax.dynamic_slice_in_dim(flat_patch, space_no * patch_rows, patch_rows, axis=1)
    weight_grad = jnp.dot(
        own_patch.T, kept_up.reshape(-1, channels), preferred_element_type=jnp.float32
    )
    emb_rows = FREQ // space_count
    own_features = lax.dynamic_slice_in_dim(features, space_no * emb_rows, emb_rows, axis=1)
    emb_grad = jnp.dot(
        own_features.T,
        jnp.concatenate([d_scales, d_shifts], axis=1),
        precision=lax.Precision.HIGHEST,
    )
    return reduce_grads(weight_grad, d_gains, emb_grad)


def reduce_grads(weight_grad, gain_grad, emb_grad):
    channels = gain_grad.shape[0]
    parts = [weight_grad, emb_grad.reshape(-1, channels), gain_grad[None]]
    rows = sum((part.shape[0] for part in parts))
    devices = lax.axis_size("dx") * lax.axis_size("dy")
    padded_rows = -(-rows // (8 * devices)) * 8 * devices
    parts.append(jnp.zeros((padded_rows - rows, channels), jnp.float32))
    flat = jnp.concatenate(parts, axis=0)
    for axis in ("dx", "dy"):
        flat = lax.psum_scatter(flat, axis, scatter_dimension=0, tiled=True)
    for axis in ("dy", "dx"):
        flat = lax.all_gather(flat, axis, axis=0, tiled=True)
    flat = lax.all_gather(flat, "space", axis=0)
    space_count = flat.shape[0]
    weight_rows = weight_grad.shape[0]
    emb_rows = emb_grad.size // channels
    conv = flat[:, :weight_rows].reshape(1, 3, 3, channels, channels)
    emb = flat[:, weight_rows : weight_rows + emb_rows].reshape(
        1, emb_grad.shape[0] * space_count, -1
    )
    gain = flat[0, weight_rows + emb_rows][None]
    return (conv, gain, emb)


def solution(mesh):
    dp_n = mesh.shape["dp"]
    dx_n = 4 if dp_n % 4 == 0 else 1
    mesh = Mesh(
        mesh.devices.reshape(dp_n // dx_n, dx_n, *mesh.devices.shape[1:]),
        ("dy", "dx", "section", "space"),
    )
    data = ("dy", "dx")
    in_specs = (
        P(data, "space", None, None),
        P(data),
        P(data, "space", None, None),
        P("section", None, None, None, None),
        P("section", None),
        P("section", None, None),
    )
    out_specs = (P("section", None, None, None, None), P("section", None), P("section", None, None))
    return jax.shard_map(
        per_device, mesh=mesh, in_specs=in_specs, out_specs=out_specs, check_vma=False
    )
```

profile of v0, /device:TPU:1, one launch (start us, length us, event | category | flops | bytes accessed | tf_op | source)
XLA Modules:
  0.0 301.1 jit_solution(14954645292781372341)
XLA Ops:
  8.3 12.7 %all_gather.18 = bf16[2,4,64,256]{3,2,1,0:T(8,128)(2,1)S(1)} all-gather(bf16[2,1,64,256]{3,2,1,0:T(8,128)(2,1)} %param.6), channel_id=1, replica_groups=mesh['dy'=8,'dx'=4,'section'=4,'space'=4] {'space'}, dimensions={1}, use_global_device_ids=true | all-gather | bytes 327680 | tf_op jit(solution)/shard_map/all_gather | solution.py:139
  24.6 1.5 fusion
  27.4 4.7 %collective-permute-start.3 = (bf16[2,4,64,256]{3,2,1,0:T(8,128)(2,1)}, bf16[2,4,64,256]{3,2,1,0:T(8,128)(2,1)S(1)}, u32[]{:S(2)}, u32[]{:S(2)}) collective-permute-start(bf16[2,4,64,256]{3,2,1,0:T(8,128)(2,1)} %fusion), channel_id=1, source_target_pairs={{0,12},{1,13},{2,14},{3,15},{16,28},{17,29},{18,30},{19,31},{32,44... | collective-permute-start | bytes 786440 | tf_op jit(solution)/shard_map/ppermute | solution.py:164
  32.1 10.7 %all_gather.19 = bf16[2,4,64,256]{3,2,1,0:T(8,128)(2,1)S(1)} all-gather(bf16[2,1,64,256]{3,2,1,0:T(8,128)(2,1)S(1)} %copy-done.7), channel_id=1, replica_groups=mesh['dy'=8,'dx'=4,'section'=4,'space'=4] {'space'}, dimensions={1}, use_global_device_ids=true | all-gather | bytes 327680 | tf_op jit(solution)/shard_map/all_gather | solution.py:140
  54.2 1.5 fusion.2
  57.7 1.6 copy.9
  61.9 2.3 fusion.28
  68.2 3.3 %fusion.23 = (f32[2,256]{1,0:T(2,128)}, f32[256]{0:T(256)}, f32[2,256]{1,0:T(2,128)S(1)}, f32[2,256]{1,0:T(2,128)S(1)}, f32[2,256]{1,0:T(2,128)}, /*index=5*/f32[2,4,64,256]{3,2,1,0:T(8,128)S(1)}) fusion(bf16[2,4,64,256]{3,2,1,0:T(8,128)(2,1)S(1)} %select_select_fusion.1, f32[2,256]{1,0:T(2,128)S(1)} %mul.236, f32[2,256]{1,0:T(2,128)} %sub.58, ...), kind=kOutput, calls=%fused_computation.105 | convolution fusion | flops 607254272 | bytes 4343808 | tf_op jit(solution)/shard_map/dot_general | solution.py:71
  74.2 1.7 fusion.22
  77.2 1.4 reduce_sum.453
  80.0 1.4 reduce_sum.455
  83.4 1.4 add.223
  86.2 1.4 mul.509
  89.2 1.5 collective-permute-start.7
  91.2 2.4 fusion.21
  100.0 1.4 mul.228
  104.9 13.3 %collective-permute-done.6 = bf16[2,4,64,256]{3,2,1,0:T(8,128)(2,1)} collective-permute-done((bf16[2,4,64,256]{3,2,1,0:T(8,128)(2,1)S(1)}, bf16[2,4,64,256]{3,2,1,0:T(8,128)(2,1)}, u32[]{:S(2)}, u32[]{:S(2)}) %collective-permute-start.6) | collective-permute-done | bytes 262176 | tf_op jit(solution)/shard_map/ppermute | solution.py:175
  124.5 1.8 fusion.17
  127.5 36.3 %reduce-scatter.3.cloned.1.call-done = f32[192,256]{1,0:T(8,128)} async-done(((f32[768,256]{1,0:T(8,128)}), f32[192,256]{1,0:T(8,128)}) %reduce-scatter.3.cloned.1.call-update) | async-done | bytes 196624 | tf_op jit(solution)/shard_map/reduce_scatter | solution.py:216
  163.9 37.1 %reduce-scatter.5.cloned.1.call-done = f32[24,256]{1,0:T(8,128)} async-done(((f32[192,256]{1,0:T(8,128)}), f32[24,256]{1,0:T(8,128)}) %reduce-scatter.5.cloned.1.call-update) | async-done | bytes 24592 | tf_op jit(solution)/shard_map/reduce_scatter | solution.py:216
  201.0 19.2 %all_gather.20 = f32[192,256]{1,0:T(8,128)S(1)} all-gather(f32[24,256]{1,0:T(8,128)} %reduce-scatter.5.cloned.1.call-done), channel_id=1, replica_groups=mesh['dy'=8,'dx'=4,'section'=4,'space'=4] {'dy'}, dimensions={0}, use_global_device_ids=true | all-gather | bytes 221184 | tf_op jit(solution)/shard_map/all_gather | solution.py:218
  220.2 11.6 %all_gather.21 = f32[768,256]{1,0:T(8,128)} all-gather(f32[192,256]{1,0:T(8,128)S(1)} %all_gather.20), channel_id=1, replica_groups=mesh['dy'=8,'dx'=4,'section'=4,'space'=4] {'dx'}, dimensions={0}, use_global_device_ids=true | all-gather | bytes 983040 | tf_op jit(solution)/shard_map/all_gather | solution.py:218
  231.7 56.3 %all-gather.3.cloned.1.call-done = f32[3072,256]{1,0:T(8,128)} async-done(((f32[768,256]{1,0:T(8,128)}), f32[3072,256]{1,0:T(8,128)}) %all-gather.3.cloned.1.call-update) | async-done | bytes 3145744 | tf_op jit(solution)/shard_map/all_gather | solution.py:219
  288.1 3.2 %slice.298 = f32[4,576,256]{2,1,0:T(8,128)} slice(f32[4,768,256]{2,1,0:T(8,128)} %bitcast.40), slice={[0:4], [0:576], [0:256]} | slice | bytes 4718592 | tf_op jit(solution)/shard_map/slice | solution.py:223
  (266 shorter events, 56.3 us)
Async XLA Ops:
  7.2 16.4 %copy-start.6 = (f32[1,256]{1,0:T(1,128)S(1)}, f32[1,256]{1,0:T(1,128)}, u32[]{:S(2)}) copy-start(f32[1,256]{1,0:T(1,128)} %param.10) | copy-start | bytes 3076
  7.2 156.6 %reduce-scatter.3.cloned.1.call-start = ((), (), s32[]{:S(2)}) async-start(), calls=%async_computation.2 | async-start | bytes 983040 | tf_op jit(solution)/shard_map/reduce_scatter | solution.py:216
  8.0 13.1 %copy-start.15 = (f32[2,128]{1,0:T(2,128)}, f32[2,128]{1,0:T(2,128)S(1)}, u32[]{:S(2)}) copy-start(f32[2,128]{1,0:T(2,128)S(1)} %get-tuple-element.52) | copy-start | bytes 3076
  8.0 13.1 %copy-start.17 = (f32[2,128]{1,0:T(2,128)}, f32[2,128]{1,0:T(2,128)S(1)}, u32[]{:S(2)}) copy-start(f32[2,128]{1,0:T(2,128)S(1)} %get-tuple-element.53) | copy-start | bytes 3076
  24.0 8.1 %copy-start.7 = (bf16[2,1,64,256]{3,2,1,0:T(8,128)(2,1)S(1)}, bf16[2,1,64,256]{3,2,1,0:T(8,128)(2,1)}, u32[]{:S(2)}) copy-start(bf16[2,1,64,256]{3,2,1,0:T(8,128)(2,1)} %param.8) | copy-start | bytes 196612
  26.1 19.0 %collective-permute-start = (bf16[2,4,64,256]{3,2,1,0:T(8,128)(2,1)}, bf16[2,4,64,256]{3,2,1,0:T(8,128)(2,1)S(1)}, u32[]{:S(2)}, u32[]{:S(2)}) collective-permute-start(bf16[2,4,64,256]{3,2,1,0:T(8,128)(2,1)} %fusion), channel_id=1, source_target_pairs={{0,4},{1,5},{2,6},{3,7},{16,20},{17,21},{18,22},{19,23},{32,36},{3... | collective-permute-start | bytes 786440 | tf_op jit(solution)/shard_map/ppermute | solution.py:159
  27.4 34.5 %collective-permute-start.3 = (bf16[2,4,64,256]{3,2,1,0:T(8,128)(2,1)}, bf16[2,4,64,256]{3,2,1,0:T(8,128)(2,1)S(1)}, u32[]{:S(2)}, u32[]{:S(2)}) collective-permute-start(bf16[2,4,64,256]{3,2,1,0:T(8,128)(2,1)} %fusion), channel_id=1, source_target_pairs={{0,12},{1,13},{2,14},{3,15},{16,28},{17,29},{18,30},{19,31},{32,44... | collective-permute-start | bytes 786440 | tf_op jit(solution)/shard_map/ppermute | solution.py:164
  47.9 2.9 collective-permute-start.1
  55.6 6.3 %collective-permute-start.2 = (bf16[2,4,64,256]{3,2,1,0:T(8,128)(2,1)}, bf16[2,4,64,256]{3,2,1,0:T(8,128)(2,1)}, u32[]{:S(2)}, u32[]{:S(2)}) collective-permute-start(bf16[2,4,64,256]{3,2,1,0:T(8,128)(2,1)} %fusion.2), channel_id=1, source_target_pairs={{8,12},{9,13},{10,14},{11,15},{24,28},{25,29},{26,30},{27,31},{40,... | collective-permute-start | bytes 786440 | tf_op jit(solution)/shard_map/ppermute | solution.py:159
  59.3 6.6 %copy-start.20 = (f32[2,32]{1,0:T(2,128)S(1)}, f32[2,32]{1,0:T(2,128)}, u32[]{:S(2)}) copy-start(f32[2,32]{1,0:T(2,128)} %copy-done.19) | copy-start | bytes 772
  60.4 7.8 %copy-start.2 = (bf16[3,3,256,256]{2,3,1,0:T(8,128)(2,1)S(1)}, bf16[3,3,256,256]{2,3,1,0:T(8,128)(2,1)}, u32[]{:S(2)}) copy-start(bf16[3,3,256,256]{2,3,1,0:T(8,128)(2,1)} %rev.3) | copy-start | bytes 3538948
  68.2 3.7 %copy-start.9 = (f32[2,32]{1,0:T(2,128)S(1)}, f32[2,32]{1,0:T(2,128)}, u32[]{:S(2)}) copy-start(f32[2,32]{1,0:T(2,128)} %copy-done.8) | copy-start | bytes 772
  68.2 3.7 %copy-start.26 = (f32[2,32]{1,0:T(2,128)S(1)}, f32[2,32]{1,0:T(2,128)}, u32[]{:S(2)}) copy-start(f32[2,32]{1,0:T(2,128)} %get-tuple-element.34) | copy-start | bytes 772
  73.0 0.7 collective-permute-start.4
  88.5 2.2 collective-permute-start.5
  89.2 15.7 %collective-permute-start.7 = (bf16[2,4,64,256]{3,2,1,0:T(8,128)(2,1)}, bf16[2,4,64,256]{3,2,1,0:T(8,128)(2,1)}, u32[]{:S(2)}, u32[]{:S(2)}) collective-permute-start(bf16[2,4,64,256]{3,2,1,0:T(8,128)(2,1)} %copy-done.5), channel_id=1, source_target_pairs={{12,0},{13,1},{14,2},{15,3},{28,16},{29,17},{30,18},{31,19},{44,32... | collective-permute-start | bytes 786440 | tf_op jit(solution)/shard_map/ppermute | solution.py:184
  91.1 2.8 copy-start.10
  96.7 21.4 %collective-permute-start.6 = (bf16[2,4,64,256]{3,2,1,0:T(8,128)(2,1)S(1)}, bf16[2,4,64,256]{3,2,1,0:T(8,128)(2,1)}, u32[]{:S(2)}, u32[]{:S(2)}) collective-permute-start(bf16[2,4,64,256]{3,2,1,0:T(8,128)(2,1)S(1)} %fusion.59), channel_id=1, source_target_pairs={{4,0},{5,1},{6,2},{7,3},{20,16},{21,17},{22,18},{23,19},{36,32},{3... | collective-permute-start | bytes 786440 | tf_op jit(solution)/shard_map/ppermute | solution.py:175
  122.3 4.0 %copy-start.38 = (f32[256]{0:T(256)S(1)}, f32[256]{0:T(256)}, u32[]{:S(2)}) copy-start(f32[256]{0:T(256)} %get-tuple-element.4) | copy-start | bytes 3076
  122.3 4.0 %copy-start.39 = (f32[256]{0:T(256)S(1)}, f32[256]{0:T(256)}, u32[]{:S(2)}) copy-start(f32[256]{0:T(256)} %get-tuple-element.7) | copy-start | bytes 3076
  122.3 4.0 %copy-start.40 = (f32[256]{0:T(256)S(1)}, f32[256]{0:T(256)}, u32[]{:S(2)}) copy-start(f32[256]{0:T(256)} %get-tuple-element.10) | copy-start | bytes 3076
  122.3 4.0 %copy-start.12 = (f32[768]{0:T(1024)S(1)}, f32[768]{0:T(1024)}, u32[]{:S(2)}) copy-start(f32[768]{0:T(1024)} %pad.36.clone) | copy-start | bytes 9220
  127.4 73.5 %reduce-scatter.5.cloned.1.call-start = ((), (), s32[]{:S(2)}) async-start(), calls=%async_computation.3 | async-start | bytes 221184 | tf_op jit(solution)/shard_map/reduce_scatter | solution.py:216
  163.8 124.2 %all-gather.3.cloned.1.call-start = ((), (), s32[]{:S(2)}) async-start(), calls=%async_computation.4 | async-start | bytes 3932160 | tf_op jit(solution)/shard_map/all_gather | solution.py:219
  (28 other events, 31.2 us)
Sparse Core Ops, SparseCore 0:
  127.6 36.1 reduce-scatter.2
  166.6 34.3 reduce-scatter.4
  231.9 56.1 all-gather.2
where the time goes:
time: 302 us; the launch traced here: 301 us
  waiting for transfers between devices  144 us (48%)
  blocking collectives  54.2 us (18%)
  local copies, waits for them, and re-layouts  43.6 us (14%)
  other arithmetic  17.7 us (6%)
  between operations  15 us (5%)
  matrix products  14.7 us (5%)
  starting transfers between devices  12.2 us (4%)
    reduce_scatter x2, waiting for transfers between devices, reduce_grads(): flat = lax.psum_scatter(flat, axis, scatter_dimension=0, tiled=True)  73.4 us
    all_gather x1, waiting for transfers between devices, reduce_grads(): flat = lax.all_gather(flat, 'space', axis=0)  56.3 us
    all_gather x2, blocking collectives, reduce_grads(): flat = lax.all_gather(flat, axis, axis=0, tiled=True)  30.7 us
    unnamed x144, local copies, waits for them, and re-layouts  14.3 us
    ppermute x3, waiting for transfers between devices, per_device(): upstream = lax.ppermute(carried, 'section', [(active + 1, active)])  13.3 us
    all_gather x1, blocking collectives, per_device(): images = lax.all_gather(images, 'space', axis=1, tiled=True)  12.7 us
    dot_general x7, matrix products, convolve(): jnp.dot(flat, matrix, preferred_element_type=jnp.float32)  12.3 us
    all_gather x1, blocking collectives, per_device(): out_grad = lax.all_gather(out_grad, 'space', axis=1, tiled=True)  10.7 us
  transfers between devices with their start and end apart: 11, of which 5 were waited for; matrix products, arithmetic and copies ran while one was open for 9% of the time, Pallas kernels for 0%

commit v1 on v0

--- a/solution.py
+++ b/solution.py
@@ -134,9 +134,18 @@
 
 
 def per_device(images, steps, out_grad, conv_weight, gn_gain, emb_weight):
+
+    def bind_tails(mat):
+        return jnp.concatenate(
+            lax.all_to_all(
+                jnp.stack([mat for _ in range(lax.axis_size("space"))], 0), "space", 0, 0
+            ),
+            1,
+        )
+
     section_count = lax.axis_size("section")
     section_no = lax.axis_index("section")
-    images = lax.all_gather(images, "space", axis=1, tiled=True)
+    images = bind_tails(images)
     out_grad = lax.all_gather(out_grad, "space", axis=1, tiled=True)
     row_count = images.shape[1]
     col_count = images.shape[2]

time: 302 us -> 305 us (level)
  blocking collectives: 54.2 us -> 38.2 us
  waiting for transfers between devices: 144 us -> 153 us
  starting transfers between devices: 12.2 us -> 19.1 us
    all_gather x1 -> x0, blocking collectives: 12.7 us -> none  [per_device(): images = lax.all_gather(images, 'space', axis=1, tiled=True)]
    all_to_all x0 -> x1, starting transfers between devices: none -> 10.3 us  [bind_tails(): lax.all_to_all(jnp.stack([mat for _ in range(lax.axis_size('space'))], 0)...]
    ppermute x1, waiting for transfers between devices: 0.65 us -> 5.57 us  [per_device(): skip_grad = lax.ppermute(d_input, 'section', [(last, 0)])]
    ppermute x3, waiting for transfers between devices: 0.01 us -> 3.89 us  [per_device(): inputs = lax.ppermute(carried, 'section', [(moment - 1, moment)])]
    ppermute x1, starting transfers between devices: 4.67 us -> 1.29 us  [per_device(): skip = lax.ppermute(output, 'section', [(0, last)])]
    all_gather x1, blocking collectives: 10.7 us -> 7.45 us  [per_device(): out_grad = lax.all_gather(out_grad, 'space', axis=1, tiled=True)]
  transfers between devices with their start and end apart: 11 -> 12, of which waited for: 5 -> 6; matrix products, arithmetic and copies ran while one was open for 9% -> 9% of each run, Pallas kernels for 0% -> 0%
where the time goes in v1:
time: 305 us; the launch traced here: 304 us
  waiting for transfers between devices  153 us (50%)
  local copies, waits for them, and re-layouts  45.3 us (15%)
  blocking collectives  38.2 us (13%)
  starting transfers between devices  19.1 us (6%)
  other arithmetic  17.7 us (6%)
  matrix products  15.3 us (5%)
  between operations  15 us (5%)
    reduce_scatter x2, waiting for transfers between devices, reduce_grads(): flat = lax.psum_scatter(flat, axis, scatter_dimension=0, tiled=True)  74.1 us
    all_gather x1, waiting for transfers between devices, reduce_grads(): flat = lax.all_gather(flat, 'space', axis=0)  56.4 us
    all_gather x2, blocking collectives, reduce_grads(): flat = lax.all_gather(flat, axis, axis=0, tiled=True)  30.8 us
    unnamed x144, local copies, waits for them, and re-layouts  14.4 us
    ppermute x3, waiting for transfers between devices, per_device(): upstream = lax.ppermute(carried, 'section', [(active + 1, active)])  13.3 us
    dot_general x7, matrix products, convolve(): jnp.dot(flat, matrix, preferred_element_type=jnp.float32)  12.9 us
    all_to_all x1, starting transfers between devices, bind_tails(): lax.all_to_all(jnp.stack([mat for _ in range(lax.axis_size('space'))], 0)...  10.3 us
    all_gather x1, blocking collectives, per_device(): out_grad = lax.all_gather(out_grad, 'space', axis=1, tiled=True)  7.45 us
  transfers between devices with their start and end apart: 12, of which 6 were waited for; matrix products, arithmetic and copies ran while one was open for 9% of the time, Pallas kernels for 0%

profile of v1, /device:TPU:1, one launch (start us, length us, event | category | flops | bytes accessed | tf_op | source)
XLA Modules:
  0.0 303.9 jit_solution(2340435281770882576)
XLA Ops:
  7.2 1.6 stack.2
  8.8 10.3 %all-to-all-start = ((bf16[4,2,1,64,256]{4,3,1,2,0:T(8,128)(2,1)}), bf16[4,2,1,64,256]{4,3,1,2,0:T(8,128)(2,1)S(1)}, u32[]{:S(2)}, u32[]{:S(2)}) async-start(bf16[4,2,1,64,256]{4,3,1,2,0:T(8,128)(2,1)} %stack.2), calls=%async_computation | async-start | bytes 524288 | tf_op jit(solution)/shard_map/all_to_all | solution.py:140
  19.7 7.5 %all_gather.15 = bf16[2,4,64,256]{3,2,1,0:T(8,128)(2,1)S(1)} all-gather(bf16[2,1,64,256]{3,2,1,0:T(8,128)(2,1)} %param.8), channel_id=1, replica_groups=mesh['dy'=8,'dx'=4,'section'=4,'space'=4] {'space'}, dimensions={1}, use_global_device_ids=true | all-gather | bytes 327680 | tf_op jit(solution)/shard_map/all_gather | solution.py:149
  31.3 1.5 fusion
  36.3 3.9 %collective-permute-done = bf16[2,4,64,256]{3,2,1,0:T(8,128)(2,1)S(1)} collective-permute-done((bf16[2,4,64,256]{3,2,1,0:T(8,128)(2,1)}, bf16[2,4,64,256]{3,2,1,0:T(8,128)(2,1)S(1)}, u32[]{:S(2)}, u32[]{:S(2)}) %collective-permute-start) | collective-permute-done | bytes 262176 | tf_op jit(solution)/shard_map/ppermute | solution.py:168
  50.7 1.5 fusion.2
  54.3 1.6 copy.11
  58.4 2.3 fusion.33
  64.7 3.3 %fusion.28 = (f32[2,256]{1,0:T(2,128)}, f32[256]{0:T(256)}, f32[2,256]{1,0:T(2,128)S(1)}, f32[2,256]{1,0:T(2,128)S(1)}, f32[2,256]{1,0:T(2,128)}, /*index=5*/f32[2,4,64,256]{3,2,1,0:T(8,128)S(1)}) fusion(bf16[2,4,64,256]{3,2,1,0:T(8,128)(2,1)S(1)} %fusion.118, f32[2,256]{1,0:T(2,128)S(1)} %mul.236, f32[2,256]{1,0:T(2,128)} %sub.58, f32[256]{0:T(256)S(1)} %bitcast.74, ...), kind=kOutput, calls=%fused_computation.110 | convolution fusion | flops 607254272 | bytes 4343808 | tf_op jit(solution)/shard_map/dot_general | solution.py:71
  70.7 1.7 fusion.27
  79.9 1.4 add.223
  85.7 1.5 collective-permute-start.7
  87.7 2.4 fusion.26
  96.5 1.4 mul.228
  100.7 5.6 %collective-permute-done.7 = bf16[2,4,64,256]{3,2,1,0:T(8,128)(2,1)} collective-permute-done((bf16[2,4,64,256]{3,2,1,0:T(8,128)(2,1)}, bf16[2,4,64,256]{3,2,1,0:T(8,128)(2,1)}, u32[]{:S(2)}, u32[]{:S(2)}) %collective-permute-start.7) | collective-permute-done | bytes 262176 | tf_op jit(solution)/shard_map/ppermute | solution.py:193
  106.3 13.3 %collective-permute-done.6 = bf16[2,4,64,256]{3,2,1,0:T(8,128)(2,1)} collective-permute-done((bf16[2,4,64,256]{3,2,1,0:T(8,128)(2,1)S(1)}, bf16[2,4,64,256]{3,2,1,0:T(8,128)(2,1)}, u32[]{:S(2)}, u32[]{:S(2)}) %collective-permute-start.6) | collective-permute-done | bytes 262176 | tf_op jit(solution)/shard_map/ppermute | solution.py:184
  121.7 1.7 fusion.25
  126.5 1.8 fusion.17
  129.5 37.0 %reduce-scatter.3.cloned.1.call-done = f32[192,256]{1,0:T(8,128)} async-done(((f32[768,256]{1,0:T(8,128)}), f32[192,256]{1,0:T(8,128)}) %reduce-scatter.3.cloned.1.call-update) | async-done | bytes 196624 | tf_op jit(solution)/shard_map/reduce_scatter | solution.py:225
  166.6 37.1 %reduce-scatter.5.cloned.1.call-done = f32[24,256]{1,0:T(8,128)} async-done(((f32[192,256]{1,0:T(8,128)}), f32[24,256]{1,0:T(8,128)}) %reduce-scatter.5.cloned.1.call-update) | async-done | bytes 24592 | tf_op jit(solution)/shard_map/reduce_scatter | solution.py:225
  203.7 19.2 %all_gather.16 = f32[192,256]{1,0:T(8,128)S(1)} all-gather(f32[24,256]{1,0:T(8,128)} %reduce-scatter.5.cloned.1.call-done), channel_id=1, replica_groups=mesh['dy'=8,'dx'=4,'section'=4,'space'=4] {'dy'}, dimensions={0}, use_global_device_ids=true | all-gather | bytes 221184 | tf_op jit(solution)/shard_map/all_gather | solution.py:227
  222.8 11.6 %all_gather.17 = f32[768,256]{1,0:T(8,128)} all-gather(f32[192,256]{1,0:T(8,128)S(1)} %all_gather.16), channel_id=1, replica_groups=mesh['dy'=8,'dx'=4,'section'=4,'space'=4] {'dx'}, dimensions={0}, use_global_device_ids=true | all-gather | bytes 983040 | tf_op jit(solution)/shard_map/all_gather | solution.py:227
  234.5 56.4 %all-gather.3.cloned.1.call-done = f32[3072,256]{1,0:T(8,128)} async-done(((f32[768,256]{1,0:T(8,128)}), f32[3072,256]{1,0:T(8,128)}) %all-gather.3.cloned.1.call-update) | async-done | bytes 3145744 | tf_op jit(solution)/shard_map/all_gather | solution.py:228
  290.9 3.2 %slice.298 = f32[4,576,256]{2,1,0:T(8,128)} slice(f32[4,768,256]{2,1,0:T(8,128)} %bitcast.55), slice={[0:4], [0:576], [0:256]} | slice | bytes 4718592 | tf_op jit(solution)/shard_map/slice | solution.py:232
  (268 shorter events, 60.2 us)
Async XLA Ops:
  7.2 20.1 %copy-start = (bf16[1,256,512]{2,1,0:T(8,128)(2,1)S(1)}, bf16[1,256,512]{2,1,0:T(8,128)(2,1)}, u32[]{:S(2)}) copy-start(bf16[1,256,512]{2,1,0:T(8,128)(2,1)} %param.11) | copy-start | bytes 786436
  7.2 23.1 %copy-start.6 = (f32[1,256]{1,0:T(1,128)S(1)}, f32[1,256]{1,0:T(1,128)}, u32[]{:S(2)}) copy-start(f32[1,256]{1,0:T(1,128)} %param.10) | copy-start | bytes 3076
  8.8 18.7 %all-to-all-start = ((bf16[4,2,1,64,256]{4,3,1,2,0:T(8,128)(2,1)}), bf16[4,2,1,64,256]{4,3,1,2,0:T(8,128)(2,1)S(1)}, u32[]{:S(2)}, u32[]{:S(2)}) async-start(bf16[4,2,1,64,256]{4,3,1,2,0:T(8,128)(2,1)} %stack.2), calls=%async_computation | async-start | bytes 524288 | tf_op jit(solution)/shard_map/all_to_all | solution.py:140
  19.0 147.5 %reduce-scatter.3.cloned.1.call-start = ((), (), s32[]{:S(2)}) async-start(), calls=%async_computation.3 | async-start | bytes 983040 | tf_op jit(solution)/shard_map/reduce_scatter | solution.py:225
  32.8 7.4 %collective-permute-start = (bf16[2,4,64,256]{3,2,1,0:T(8,128)(2,1)}, bf16[2,4,64,256]{3,2,1,0:T(8,128)(2,1)S(1)}, u32[]{:S(2)}, u32[]{:S(2)}) collective-permute-start(bf16[2,4,64,256]{3,2,1,0:T(8,128)(2,1)} %fusion), channel_id=1, source_target_pairs={{0,4},{1,5},{2,6},{3,7},{16,20},{17,21},{18,22},{19,23},{32,36},{3... | collective-permute-start | bytes 786440 | tf_op jit(solution)/shard_map/ppermute | solution.py:168
  43.1 4.2 %collective-permute-start.1 = (bf16[2,4,64,256]{3,2,1,0:T(8,128)(2,1)S(1)}, bf16[2,4,64,256]{3,2,1,0:T(8,128)(2,1)S(1)}, u32[]{:S(2)}, u32[]{:S(2)}) collective-permute-start(bf16[2,4,64,256]{3,2,1,0:T(8,128)(2,1)S(1)} %fusion.1), channel_id=1, source_target_pairs={{4,8},{5,9},{6,10},{7,11},{20,24},{21,25},{22,26},{23,27},{36,40},... | collective-permute-start | bytes 786440 | tf_op jit(solution)/shard_map/ppermute | solution.py:168
  46.0 12.4 %collective-permute-start.3 = (bf16[2,4,64,256]{3,2,1,0:T(8,128)(2,1)}, bf16[2,4,64,256]{3,2,1,0:T(8,128)(2,1)S(1)}, u32[]{:S(2)}, u32[]{:S(2)}) collective-permute-start(bf16[2,4,64,256]{3,2,1,0:T(8,128)(2,1)} %fusion), channel_id=1, source_target_pairs={{0,12},{1,13},{2,14},{3,15},{16,28},{17,29},{18,30},{19,31},{32,44... | collective-permute-start | bytes 786440 | tf_op jit(solution)/shard_map/ppermute | solution.py:173
  52.2 6.3 %collective-permute-start.2 = (bf16[2,4,64,256]{3,2,1,0:T(8,128)(2,1)}, bf16[2,4,64,256]{3,2,1,0:T(8,128)(2,1)}, u32[]{:S(2)}, u32[]{:S(2)}) collective-permute-start(bf16[2,4,64,256]{3,2,1,0:T(8,128)(2,1)} %fusion.2), channel_id=1, source_target_pairs={{8,12},{9,13},{10,14},{11,15},{24,28},{25,29},{26,30},{27,31},{40,... | collective-permute-start | bytes 786440 | tf_op jit(solution)/shard_map/ppermute | solution.py:168
  55.8 6.6 %copy-start.19 = (f32[2,32]{1,0:T(2,128)S(1)}, f32[2,32]{1,0:T(2,128)}, u32[]{:S(2)}) copy-start(f32[2,32]{1,0:T(2,128)} %copy-done.18) | copy-start | bytes 772
  56.9 7.8 %copy-start.2 = (bf16[3,3,256,256]{2,3,1,0:T(8,128)(2,1)S(1)}, bf16[3,3,256,256]{2,3,1,0:T(8,128)(2,1)}, u32[]{:S(2)}) copy-start(bf16[3,3,256,256]{2,3,1,0:T(8,128)(2,1)} %rev.3) | copy-start | bytes 3538948
  64.7 3.7 %copy-start.8 = (f32[2,32]{1,0:T(2,128)S(1)}, f32[2,32]{1,0:T(2,128)}, u32[]{:S(2)}) copy-start(f32[2,32]{1,0:T(2,128)} %copy-done.7) | copy-start | bytes 772
  64.7 3.7 %copy-start.25 = (f32[2,32]{1,0:T(2,128)S(1)}, f32[2,32]{1,0:T(2,128)}, u32[]{:S(2)}) copy-start(f32[2,32]{1,0:T(2,128)} %get-tuple-element.34) | copy-start | bytes 772
  69.5 0.7 collective-permute-start.4
  85.0 2.2 collective-permute-start.5
  85.7 20.6 %collective-permute-start.7 = (bf16[2,4,64,256]{3,2,1,0:T(8,128)(2,1)}, bf16[2,4,64,256]{3,2,1,0:T(8,128)(2,1)}, u32[]{:S(2)}, u32[]{:S(2)}) collective-permute-start(bf16[2,4,64,256]{3,2,1,0:T(8,128)(2,1)} %copy-done.5), channel_id=1, source_target_pairs={{12,0},{13,1},{14,2},{15,3},{28,16},{29,17},{30,18},{31,19},{44,32... | collective-permute-start | bytes 786440 | tf_op jit(solution)/shard_map/ppermute | solution.py:193
  87.6 2.8 copy-start.9
  93.2 26.3 %collective-permute-start.6 = (bf16[2,4,64,256]{3,2,1,0:T(8,128)(2,1)S(1)}, bf16[2,4,64,256]{3,2,1,0:T(8,128)(2,1)}, u32[]{:S(2)}, u32[]{:S(2)}) collective-permute-start(bf16[2,4,64,256]{3,2,1,0:T(8,128)(2,1)S(1)} %fusion.59), channel_id=1, source_target_pairs={{4,0},{5,1},{6,2},{7,3},{20,16},{21,17},{22,18},{23,19},{36,32},{3... | collective-permute-start | bytes 786440 | tf_op jit(solution)/shard_map/ppermute | solution.py:184
  124.3 4.0 %copy-start.37 = (f32[256]{0:T(256)S(1)}, f32[256]{0:T(256)}, u32[]{:S(2)}) copy-start(f32[256]{0:T(256)} %get-tuple-element.4) | copy-start | bytes 3076
  124.3 4.0 %copy-start.38 = (f32[256]{0:T(256)S(1)}, f32[256]{0:T(256)}, u32[]{:S(2)}) copy-start(f32[256]{0:T(256)} %get-tuple-element.7) | copy-start | bytes 3076
  124.3 4.0 %copy-start.39 = (f32[256]{0:T(256)S(1)}, f32[256]{0:T(256)}, u32[]{:S(2)}) copy-start(f32[256]{0:T(256)} %get-tuple-element.10) | copy-start | bytes 3076
  124.3 4.0 %copy-start.40 = (f32[256]{0:T(256)S(1)}, f32[256]{0:T(256)}, u32[]{:S(2)}) copy-start(f32[256]{0:T(256)} %get-tuple-element.13) | copy-start | bytes 3076
  124.3 4.0 %copy-start.11 = (f32[768]{0:T(1024)S(1)}, f32[768]{0:T(1024)}, u32[]{:S(2)}) copy-start(f32[768]{0:T(1024)} %pad.36.clone) | copy-start | bytes 9220
  129.5 74.2 %reduce-scatter.5.cloned.1.call-start = ((), (), s32[]{:S(2)}) async-start(), calls=%async_computation.4 | async-start | bytes 221184 | tf_op jit(solution)/shard_map/reduce_scatter | solution.py:225
  166.5 124.3 %all-gather.3.cloned.1.call-start = ((), (), s32[]{:S(2)}) async-start(), calls=%async_computation.5 | async-start | bytes 3932160 | tf_op jit(solution)/shard_map/all_gather | solution.py:228
  (29 other events, 29.9 us)
Sparse Core Ops, SparseCore 0:
  129.6 36.8 reduce-scatter.2
  169.3 34.3 reduce-scatter.4
  234.6 56.2 all-gather.2
